TPU v7x, 512 devices: a whole 4x8x8 slice. The times are simulated.
512 devices in a mesh: req: 64 (over z, x, core), voc: 8 (over y).
Axes of the slice: x: 4, y: 8, z: 8, core: 2. Of those that a mesh axis runs over, the one named last changes fastest.
Arguments:
- hidden: bfloat16 [65536, 1600], P(('req', 'voc')), may hold values from -60 to 60
- norm_gain: float32 [1600], replicated, may hold values from 0.25 to 1.75
- unembed: bfloat16 [16384, 1600], P(('req', 'voc')), may hold values from -2 to 2
- targets: int32 [65536], P(('req', 'voc')), may hold values from 0 to 16383
- live: int32 [65536], P(('req', 'voc')), may hold values from 0 to 1, as said below
Outputs:
- logprob: float32 [65536], P(('req', 'voc'))
- entropy: float32 [65536], P(('req', 'voc'))
Inputs may be any that keep to these rules, and one draw needn't show every extreme that they name: Within each aligned block of 1024 slots (one owner's) the live slots form a prefix of 128 to 1024 slots, and in every draw at least one block is wholly live.
All inputs are finite; a program needn't handle non-finite values.
Results may differ from a plain program's by a relative error of at most 0.0067.
Values may be sent and summed in bfloat16 or wider, within the bound.
No kernel may reach another device: no remote copies, remote signals or barrier semaphores. Data moves between devices by JAX's collectives and lax.ppermute only.
A program may use at most 64 MiB of HBM per device.

v0:
```python
import jax
import jax.numpy as jnp
from jax import lax
from jax.sharding import Mesh, PartitionSpec as P

FLAT = ("z", "x", "c", "y")


def combine_stats(first, second):
    top = jnp.maximum(first[0], second[0])
    scale_one = jnp.exp(first[0] - top)
    scale_two = jnp.exp(second[0] - top)
    total = first[1] * scale_one + second[1] * scale_two
    spread = scale_one * (first[2] + (first[0] - top) * first[1]) + scale_two * (
        second[2] + (second[0] - top) * second[1]
    )
    return (top, total, spread, first[3] + second[3])


def shift(value, axis, size, step):
    return lax.ppermute(value, axis, [(i, (i + step) % size) for i in range(size)])


def chunk_stats(normed, piece, ids, wanted):
    logits = lax.dot_general(
        normed, piece, (((1,), (1,)), ((), ())), preferred_element_type=jnp.float32
    )
    chosen = jnp.sum(jnp.where(ids[None, :] == wanted[:, None], logits, 0.0), axis=1)
    fold_top = jnp.max(logits, axis=1)
    shifted = logits - fold_top[:, None]
    weights = jnp.exp(shifted)
    return (fold_top, jnp.sum(weights, axis=1), jnp.sum(weights * shifted, axis=1), chosen)


def on_device(hidden, norm_gain, unembed, targets, live):
    ny = lax.axis_size("y")
    nc = lax.axis_size("c")
    y = lax.axis_index("y")
    c = lax.axis_index("c")
    mine = hidden.shape[0]
    dim = hidden.shape[1]
    width = unembed.shape[0]
    wide = hidden.astype(jnp.float32)
    normed = (
        wide * lax.rsqrt(jnp.mean(wide * wide, axis=1, keepdims=True) + 1e-06) * norm_gain
    ).astype(jnp.bfloat16)
    code = jnp.zeros((mine, 16), jnp.bfloat16)
    code = code.at[:, 0].set((targets // 128).astype(jnp.bfloat16))
    code = code.at[:, 1].set((targets % 128).astype(jnp.bfloat16))
    block = jnp.concatenate([normed, code], axis=1)
    blocks = [None] * ny
    blocks[0] = block
    fwd = ny // 2
    cur = block
    for d in range(1, fwd + 1):
        cur = shift(cur, "y", ny, 1)
        blocks[ny - d] = cur
    cur = block
    for d in range(1, ny - fwd):
        cur = shift(cur, "y", ny, -1)
        blocks[d] = cur
    rows = jnp.concatenate([b[:, :dim] for b in blocks], axis=0)
    wanted = jnp.concatenate(
        [b[:, dim].astype(jnp.int32) * 128 + b[:, dim + 1].astype(jnp.int32) for b in blocks],
        axis=0,
    )
    whole = lax.all_gather(unembed, ("z", "x", "c"), axis=0, tiled=True)
    local = jnp.arange(whole.shape[0], dtype=jnp.int32)
    ids = (local // width * ny + y) * width + local % width
    count = rows.shape[0]
    zeros = jnp.zeros((count,), jnp.float32)
    stats = (jnp.full((count,), -1e30, jnp.float32), zeros, zeros, zeros)
    step = min(512, whole.shape[0])
    for first in range(0, whole.shape[0], step):
        stats = combine_stats(
            stats, chunk_stats(rows, whole[first : first + step], ids[first : first + step], wanted)
        )
    packed = jnp.roll(jnp.stack(stats).reshape(4, ny, mine), y, axis=1).reshape(4, ny * mine)
    got = lax.all_to_all(packed, "y", 1, 1, tiled=True).reshape(4, ny, mine)
    tops, totals, spreads, chosen = (got[0], got[1], got[2], got[3])
    top = jnp.max(tops, axis=0)
    scale = jnp.exp(tops - top[None])
    total = jnp.sum(totals * scale, axis=0)
    spread = jnp.sum(scale * (spreads + (tops - top[None]) * totals), axis=0)
    picked = jnp.sum(chosen, axis=0)
    mask = live.astype(jnp.float32)
    logprob = (picked - top - jnp.log(total)) * mask
    entropy = (jnp.log(total) - spread / total) * mask
    return (logprob, entropy)


def solution(mesh):
    nz, nx, nc = (8, 4, 2)
    ny = mesh.devices.shape[1]
    req = mesh.devices.shape[0]
    nz = req // (nx * nc)
    flat = Mesh(mesh.devices.reshape(nz, nx, nc, ny), FLAT)
    return jax.shard_map(
        on_device,
        mesh=flat,
        in_specs=(P(FLAT, None), P(), P(FLAT, None), P(FLAT), P(FLAT)),
        out_specs=(P(FLAT), P(FLAT)),
        check_vma=False,
    )
```

profile of v0, /device:TPU:1, one launch (start us, length us, event | category | flops | bytes accessed | tf_op | source)
XLA Modules:
  0.0 140.3 jit_solution(5805174977988451406)
XLA Ops:
  7.2 0.7 all-gather.2.cloned.1.call-update
  7.9 0.6 compare_reduce_fusion.1
  8.5 0.6 compare_reduce_fusion
  9.2 2.0 %broadcast_select_fusion = (bf16[128]{0:T(256)(128)(2,1)S(1)}, bf16[128,1]{0,1:T(2,128)(2,1)S(1)}) fusion(pred[]{:T(512)} %compare_reduce_fusion, s32[128]{0:T(128)} %param.12, pred[]{:T(512)} %compare_reduce_fusion.1), kind=kLoop, calls=%fused_computation.128 | loop fusion | flops 2944 | bytes 1026 | tf_op jit(solution)/shard_map/slice | solution.py:64
  11.2 1.2 fusion.12
  12.4 2.1 %constant_dynamic-update-slice_fusion = (bf16[1024,1600]{0,1:T(8,128)(2,1)}, bf16[128,1600]{0,1:T(8,128)(2,1)S(1)}) fusion(f32[1600]{0:T(1024)} %param.10, f32[128]{0:T(128)S(1)} %add_rsqrt_fusion, bf16[128,1600]{0,1:T(8,128)(2,1)} %param.9), kind=kLoop, calls=%fused_computation.45 | loop fusion | flops 819199 | bytes 1235712
  14.6 4.0 %collective-permute-start.3 = (bf16[128,1616]{0,1:T(8,128)(2,1)S(1)}, bf16[128,1616]{0,1:T(8,128)(2,1)S(1)}, u32[]{:S(2)}, u32[]{:S(2)}) collective-permute-start(bf16[128,1616]{0,1:T(8,128)(2,1)S(1)} %pad_maximum_fusion), channel_id=1, source_target_pairs={{0,1},{1,2},{2,3},{3,4},{4,5},{5,6},{6,7},{7,0},{8,9},{9,10},{10,1... | collective-permute-start | bytes 1241096 | tf_op jit(solution)/shard_map/ppermute | solution.py:21
  18.6 3.8 %collective-permute-start = (bf16[128,1616]{0,1:T(8,128)(2,1)S(1)}, bf16[128,1616]{0,1:T(8,128)(2,1)S(1)}, u32[]{:S(2)}, u32[]{:S(2)}) collective-permute-start(bf16[128,1616]{0,1:T(8,128)(2,1)S(1)} %pad_maximum_fusion), channel_id=1, source_target_pairs={{0,7},{1,0},{2,1},{3,2},{4,3},{5,4},{6,5},{7,6},{8,15},{9,8},{10,9... | collective-permute-start | bytes 1241096 | tf_op jit(solution)/shard_map/ppermute | solution.py:21
  22.5 3.4 %collective-permute-done.3 = bf16[128,1616]{0,1:T(8,128)(2,1)S(1)} collective-permute-done((bf16[128,1616]{0,1:T(8,128)(2,1)S(1)}, bf16[128,1616]{0,1:T(8,128)(2,1)S(1)}, u32[]{:S(2)}, u32[]{:S(2)}) %collective-permute-start.3) | collective-permute-done | bytes 413728 | tf_op jit(solution)/shard_map/ppermute | solution.py:21
  25.9 4.1 %collective-permute-start.4 = (bf16[128,1616]{0,1:T(8,128)(2,1)S(1)}, bf16[128,1616]{0,1:T(8,128)(2,1)S(1)}, u32[]{:S(2)}, u32[]{:S(2)}) collective-permute-start(bf16[128,1616]{0,1:T(8,128)(2,1)S(1)} %collective-permute-done.3), channel_id=1, source_target_pairs={{0,1},{1,2},{2,3},{3,4},{4,5},{5,6},{6,7},{7,0},{8,9},{9,10},{10,1... | collective-permute-start | bytes 1241096 | tf_op jit(solution)/shard_map/ppermute | solution.py:21
  30.0 4.7 %collective-permute-start.1 = (bf16[128,1616]{0,1:T(8,128)(2,1)S(1)}, bf16[128,1616]{0,1:T(8,128)(2,1)S(1)}, u32[]{:S(2)}, u32[]{:S(2)}) collective-permute-start(bf16[128,1616]{0,1:T(8,128)(2,1)S(1)} %collective-permute-done), channel_id=1, source_target_pairs={{0,7},{1,0},{2,1},{3,2},{4,3},{5,4},{6,5},{7,6},{8,15},{9,8},{10,9... | collective-permute-start | bytes 1241096 | tf_op jit(solution)/shard_map/ppermute | solution.py:21
  34.8 0.8 slice_dynamic-update-slice_fusion.6
  35.6 2.9 %collective-permute-done.4 = bf16[128,1616]{0,1:T(8,128)(2,1)S(1)} collective-permute-done((bf16[128,1616]{0,1:T(8,128)(2,1)S(1)}, bf16[128,1616]{0,1:T(8,128)(2,1)S(1)}, u32[]{:S(2)}, u32[]{:S(2)}) %collective-permute-start.4) | collective-permute-done | bytes 413728 | tf_op jit(solution)/shard_map/ppermute | solution.py:21
  38.5 2.9 %collective-permute-start.5 = (bf16[128,1616]{0,1:T(8,128)(2,1)S(1)}, bf16[128,1616]{0,1:T(8,128)(2,1)S(1)}, u32[]{:S(2)}, u32[]{:S(2)}) collective-permute-start(bf16[128,1616]{0,1:T(8,128)(2,1)S(1)} %collective-permute-done.4), channel_id=1, source_target_pairs={{0,1},{1,2},{2,3},{3,4},{4,5},{5,6},{6,7},{7,0},{8,9},{9,10},{10,1... | collective-permute-start | bytes 1241096 | tf_op jit(solution)/shard_map/ppermute | solution.py:21
  41.4 4.7 %collective-permute-start.2 = (bf16[128,1616]{0,1:T(8,128)(2,1)S(1)}, bf16[128,1616]{0,1:T(8,128)(2,1)S(1)}, u32[]{:S(2)}, u32[]{:S(2)}) collective-permute-start(bf16[128,1616]{0,1:T(8,128)(2,1)S(1)} %collective-permute-done.1), channel_id=1, source_target_pairs={{0,7},{1,0},{2,1},{3,2},{4,3},{5,4},{6,5},{7,6},{8,15},{9,8},{10,9... | collective-permute-start | bytes 1241096 | tf_op jit(solution)/shard_map/ppermute | solution.py:21
  46.1 0.9 slice_dynamic-update-slice_fusion.5
  47.0 2.9 %collective-permute-done.5 = bf16[128,1616]{0,1:T(8,128)(2,1)S(1)} collective-permute-done((bf16[128,1616]{0,1:T(8,128)(2,1)S(1)}, bf16[128,1616]{0,1:T(8,128)(2,1)S(1)}, u32[]{:S(2)}, u32[]{:S(2)}) %collective-permute-start.5) | collective-permute-done | bytes 413728 | tf_op jit(solution)/shard_map/ppermute | solution.py:21
  50.0 2.1 %collective-permute-start.6 = (bf16[128,1616]{0,1:T(8,128)(2,1)S(1)}, bf16[128,1616]{0,1:T(8,128)(2,1)S(1)}, u32[]{:S(2)}, u32[]{:S(2)}) collective-permute-start(bf16[128,1616]{0,1:T(8,128)(2,1)S(1)} %collective-permute-done.5), channel_id=1, source_target_pairs={{0,1},{1,2},{2,3},{3,4},{4,5},{5,6},{6,7},{7,0},{8,9},{9,10},{10,1... | collective-permute-start | bytes 1241096 | tf_op jit(solution)/shard_map/ppermute | solution.py:21
  52.1 2.0 %collective-permute-done.2 = bf16[128,1616]{0,1:T(8,128)(2,1)S(1)} collective-permute-done((bf16[128,1616]{0,1:T(8,128)(2,1)S(1)}, bf16[128,1616]{0,1:T(8,128)(2,1)S(1)}, u32[]{:S(2)}, u32[]{:S(2)}) %collective-permute-start.2) | collective-permute-done | bytes 413728 | tf_op jit(solution)/shard_map/ppermute | solution.py:21
  54.1 0.8 slice_dynamic-update-slice_fusion.4
  54.9 5.5 %collective-permute-done.6 = bf16[128,1616]{0,1:T(8,128)(2,1)S(1)} collective-permute-done((bf16[128,1616]{0,1:T(8,128)(2,1)S(1)}, bf16[128,1616]{0,1:T(8,128)(2,1)S(1)}, u32[]{:S(2)}, u32[]{:S(2)}) %collective-permute-start.6) | collective-permute-done | bytes 413728 | tf_op jit(solution)/shard_map/ppermute | solution.py:21
  60.5 0.8 slice_dynamic-update-slice_fusion.3
  61.4 0.9 slice_dynamic-update-slice_fusion.2
  62.2 0.8 slice_dynamic-update-slice_fusion.1
  63.1 0.9 slice_dynamic-update-slice_fusion
  63.9 40.9 %all-gather.2.cloned.1.call-done = bf16[2048,1600]{1,0:T(8,128)(2,1)} async-done(((bf16[32,1600]{1,0:T(8,128)(2,1)}), bf16[2048,1600]{1,0:T(8,128)(2,1)}) %all-gather.2.cloned.1.call-update) | async-done | bytes 6553616 | tf_op jit(solution)/shard_map/all_gather | solution.py:67
  104.8 4.7 %fusion.82 = (f32[1024]{0:T(1024)S(1)}, f32[1024,512]{0,1:T(8,128)S(1)}) fusion(bf16[1024,1600]{0,1:T(8,128)(2,1)} %slice_dynamic-update-slice_fusion, bf16[2048,1600]{1,0:T(8,128)(2,1)} %all-gather.2.cloned.1.call-done), kind=kOutput, calls=%fused_computation.177 | convolution fusion | flops 1678244864 | bytes 7081984 | tf_op jit(solution)/shard_map/dot_general | solution.py:25
  109.5 2.1 %fusion.83 = (f32[1024]{0:T(1024)S(1)}, f32[1024,512]{0,1:T(8,128)S(1)}) fusion(bf16[1024,1600]{0,1:T(8,128)(2,1)S(1)} %copy-done, bf16[2048,1600]{1,0:T(8,128)(2,1)S(1)} %copy-done.2), kind=kOutput, calls=%fused_computation.178 | convolution fusion | flops 1678244864 | bytes 7081984 | tf_op jit(solution)/shard_map/dot_general | solution.py:25
  111.7 2.1 %fusion.84 = (f32[1024]{0:T(1024)S(1)}, f32[1024,512]{0,1:T(8,128)S(1)}) fusion(bf16[1024,1600]{0,1:T(8,128)(2,1)S(1)} %copy-done, bf16[2048,1600]{1,0:T(8,128)(2,1)S(1)} %copy-done.2), kind=kOutput, calls=%fused_computation.179 | convolution fusion | flops 1678244864 | bytes 7081984 | tf_op jit(solution)/shard_map/dot_general | solution.py:25
  113.8 2.1 %fusion.85 = (f32[1024]{0:T(1024)S(1)}, f32[1024,512]{0,1:T(8,128)S(1)}) fusion(bf16[1024,1600]{0,1:T(8,128)(2,1)S(1)} %copy-done, bf16[2048,1600]{1,0:T(8,128)(2,1)S(1)} %copy-done.2), kind=kOutput, calls=%fused_computation.180 | convolution fusion | flops 1678244864 | bytes 7081984 | tf_op jit(solution)/shard_map/dot_general | solution.py:25
  115.9 3.9 %fusion = (f32[1024]{0:T(1024)S(1)}, f32[1024]{0:T(1024)S(1)}, f32[1024]{0:T(1024)S(1)}, f32[1024]{0:T(1024)S(1)}, f32[1024]{0:T(1024)S(1)}, /*index=5*/f32[1024...) fusion(f32[1024,512]{0,1:T(8,128)S(1)} %get-tuple-element.67, ...), kind=kLoop, calls=%fused_computation.8 | loop fusion | flops 14667776 | bytes 8466432 | tf_op jit(solution)/shard_map/reduce_sum | solution.py:32
  119.9 12.9 %all_to_all.6 = f32[4,8,128]{2,0,1:T(4,128)S(1)} all-to-all(f32[4,8,128]{2,0,1:T(4,128)S(1)} %copy.9), channel_id=1, replica_groups=mesh['z'=8,'x'=4,'c'=2,'y'=8] {'y'}, dimensions={1} | all-to-all | bytes 32768 | tf_op jit(solution)/shard_map/all_to_all | solution.py:79
  (32 shorter events, 0.9 us)
Async XLA Ops:
  7.2 97.7 %all-gather.2.cloned.1.call-start = ((), (), s32[]{:S(2)}) async-start(), calls=%async_computation.1 | async-start | bytes 6922240 | tf_op jit(solution)/shard_map/all_gather | solution.py:67
  14.6 11.3 %collective-permute-start.3 = (bf16[128,1616]{0,1:T(8,128)(2,1)S(1)}, bf16[128,1616]{0,1:T(8,128)(2,1)S(1)}, u32[]{:S(2)}, u32[]{:S(2)}) collective-permute-start(bf16[128,1616]{0,1:T(8,128)(2,1)S(1)} %pad_maximum_fusion), channel_id=1, source_target_pairs={{0,1},{1,2},{2,3},{3,4},{4,5},{5,6},{6,7},{7,0},{8,9},{9,10},{10,1... | collective-permute-start | bytes 1241096 | tf_op jit(solution)/shard_map/ppermute | solution.py:21
  18.6 11.4 %collective-permute-start = (bf16[128,1616]{0,1:T(8,128)(2,1)S(1)}, bf16[128,1616]{0,1:T(8,128)(2,1)S(1)}, u32[]{:S(2)}, u32[]{:S(2)}) collective-permute-start(bf16[128,1616]{0,1:T(8,128)(2,1)S(1)} %pad_maximum_fusion), channel_id=1, source_target_pairs={{0,7},{1,0},{2,1},{3,2},{4,3},{5,4},{6,5},{7,6},{8,15},{9,8},{10,9... | collective-permute-start | bytes 1241096 | tf_op jit(solution)/shard_map/ppermute | solution.py:21
  25.9 12.6 %collective-permute-start.4 = (bf16[128,1616]{0,1:T(8,128)(2,1)S(1)}, bf16[128,1616]{0,1:T(8,128)(2,1)S(1)}, u32[]{:S(2)}, u32[]{:S(2)}) collective-permute-start(bf16[128,1616]{0,1:T(8,128)(2,1)S(1)} %collective-permute-done.3), channel_id=1, source_target_pairs={{0,1},{1,2},{2,3},{3,4},{4,5},{5,6},{6,7},{7,0},{8,9},{9,10},{10,1... | collective-permute-start | bytes 1241096 | tf_op jit(solution)/shard_map/ppermute | solution.py:21
  30.0 11.4 %collective-permute-start.1 = (bf16[128,1616]{0,1:T(8,128)(2,1)S(1)}, bf16[128,1616]{0,1:T(8,128)(2,1)S(1)}, u32[]{:S(2)}, u32[]{:S(2)}) collective-permute-start(bf16[128,1616]{0,1:T(8,128)(2,1)S(1)} %collective-permute-done), channel_id=1, source_target_pairs={{0,7},{1,0},{2,1},{3,2},{4,3},{5,4},{6,5},{7,6},{8,15},{9,8},{10,9... | collective-permute-start | bytes 1241096 | tf_op jit(solution)/shard_map/ppermute | solution.py:21
  38.5 11.5 %collective-permute-start.5 = (bf16[128,1616]{0,1:T(8,128)(2,1)S(1)}, bf16[128,1616]{0,1:T(8,128)(2,1)S(1)}, u32[]{:S(2)}, u32[]{:S(2)}) collective-permute-start(bf16[128,1616]{0,1:T(8,128)(2,1)S(1)} %collective-permute-done.4), channel_id=1, source_target_pairs={{0,1},{1,2},{2,3},{3,4},{4,5},{5,6},{6,7},{7,0},{8,9},{9,10},{10,1... | collective-permute-start | bytes 1241096 | tf_op jit(solution)/shard_map/ppermute | solution.py:21
  41.4 12.7 %collective-permute-start.2 = (bf16[128,1616]{0,1:T(8,128)(2,1)S(1)}, bf16[128,1616]{0,1:T(8,128)(2,1)S(1)}, u32[]{:S(2)}, u32[]{:S(2)}) collective-permute-start(bf16[128,1616]{0,1:T(8,128)(2,1)S(1)} %collective-permute-done.1), channel_id=1, source_target_pairs={{0,7},{1,0},{2,1},{3,2},{4,3},{5,4},{6,5},{7,6},{8,15},{9,8},{10,9... | collective-permute-start | bytes 1241096 | tf_op jit(solution)/shard_map/ppermute | solution.py:21
  50.0 10.5 %collective-permute-start.6 = (bf16[128,1616]{0,1:T(8,128)(2,1)S(1)}, bf16[128,1616]{0,1:T(8,128)(2,1)S(1)}, u32[]{:S(2)}, u32[]{:S(2)}) collective-permute-start(bf16[128,1616]{0,1:T(8,128)(2,1)S(1)} %collective-permute-done.5), channel_id=1, source_target_pairs={{0,1},{1,2},{2,3},{3,4},{4,5},{5,6},{6,7},{7,0},{8,9},{9,10},{10,1... | collective-permute-start | bytes 1241096 | tf_op jit(solution)/shard_map/ppermute | solution.py:21
  63.9 45.6 %copy-start = (bf16[1024,1600]{0,1:T(8,128)(2,1)S(1)}, bf16[1024,1600]{0,1:T(8,128)(2,1)}, u32[]{:S(2)}) copy-start(bf16[1024,1600]{0,1:T(8,128)(2,1)} %slice_dynamic-update-slice_fusion) | copy-start | bytes 9830404
  104.8 4.7 %copy-start.2 = (bf16[2048,1600]{1,0:T(8,128)(2,1)S(1)}, bf16[2048,1600]{1,0:T(8,128)(2,1)}, u32[]{:S(2)}) copy-start(bf16[2048,1600]{1,0:T(8,128)(2,1)} %all-gather.2.cloned.1.call-done) | copy-start | bytes 19660804
  115.9 17.0 %copy-start.1 = (s32[128]{0:T(128)S(1)}, s32[128]{0:T(128)}, u32[]{:S(2)}) copy-start(s32[128]{0:T(128)} %param.13) | copy-start | bytes 1540
Sparse Core Ops, SparseCore 0:
  11.3 93.4 all-gather.1
where the time goes:
time: 141 us; the launch traced here: 140 us
  waiting for transfers between devices  58.4 us (41%)
  starting transfers between devices  26.4 us (19%)
  between operations  14.3 us (10%)
  blocking collectives  12.9 us (9%)
  other arithmetic  11.3 us (8%)
  matrix products  11 us (8%)
  local copies, waits for them, and re-layouts  5.97 us (4%)
    all_gather x1, waiting for transfers between devices, on_device(): whole = lax.all_gather(unembed, ('z', 'x', 'c'), axis=0, tiled=True)  40.9 us
    ppermute x7, starting transfers between devices, shift(): lax.ppermute(value, axis, [(i, (i + step) % size) for i in range(size)])  26.4 us
    ppermute x7, waiting for transfers between devices, shift(): lax.ppermute(value, axis, [(i, (i + step) % size) for i in range(size)])  16.8 us
    all_to_all x1, blocking collectives, on_device(): got = lax.all_to_all(packed, 'y', 1, 1, tiled=True).reshape(4, ny, mine)  12.9 us
    dot_general x4, matrix products, chunk_stats(): lax.dot_general(normed, piece, (((1,), (1,)), ((), ())), preferred_elemen...  11 us
    unnamed x12, local copies, waits for them, and re-layouts  5.05 us
    reduce_sum x1, other arithmetic, chunk_stats(): jnp.sum(weights * shifted, axis=1)  3.9 us
  transfers between devices with their start and end apart: 8, of which 6 were waited for; matrix products, arithmetic and copies ran while one was open for 9% of the time, Pallas kernels for 0%

commit v1 on v0

--- a/solution.py
+++ b/solution.py
@@ -2,6 +2,7 @@
 import jax.numpy as jnp
 from jax import lax
 from jax.sharding import Mesh, PartitionSpec as P
+from jax.lax import all_to_all, axis_size
 
 FLAT = ("z", "x", "c", "y")
 
@@ -76,7 +77,16 @@
             stats, chunk_stats(rows, whole[first : first + step], ids[first : first + step], wanted)
         )
     packed = jnp.roll(jnp.stack(stats).reshape(4, ny, mine), y, axis=1).reshape(4, ny * mine)
-    got = lax.all_to_all(packed, "y", 1, 1, tiled=True).reshape(4, ny, mine)
+    post_case_in = lambda obj, d0, in_dim: jnp.concatenate(
+        all_to_all(
+            jnp.stack(jnp.split(obj, axis_size("y"), axis=d0), 0),
+            axis_name="y",
+            split_axis=0,
+            concat_axis=0,
+        ),
+        axis=in_dim,
+    )
+    got = post_case_in(packed, 1, 1).reshape(4, ny, mine)
     tops, totals, spreads, chosen = (got[0], got[1], got[2], got[3])
     top = jnp.max(tops, axis=0)
     scale = jnp.exp(tops - top[None])

time: 141 us -> 141 us (level)
    unnamed x12 -> x20, local copies, waits for them, and re-layouts: 5.05 us -> 5.12 us
where the time goes in v1:
time: 141 us; the launch traced here: 140 us
  waiting for transfers between devices  58.4 us (41%)
  starting transfers between devices  26.4 us (19%)
  between operations  14.3 us (10%)
  blocking collectives  12.9 us (9%)
  other arithmetic  11.3 us (8%)
  matrix products  11 us (8%)
  local copies, waits for them, and re-layouts  6.04 us (4%)
    all_gather x1, waiting for transfers between devices, on_device(): whole = lax.all_gather(unembed, ('z', 'x', 'c'), axis=0, tiled=True)  40.9 us
    ppermute x7, starting transfers between devices, shift(): lax.ppermute(value, axis, [(i, (i + step) % size) for i in range(size)])  26.4 us
    ppermute x7, waiting for transfers between devices, shift(): lax.ppermute(value, axis, [(i, (i + step) % size) for i in range(size)])  16.8 us
    all_to_all x1, blocking collectives, on_device(): all_to_all(jnp.stack(jnp.split(obj, axis_size('y'), axis=d0), 0), axis_na...  12.9 us
    dot_general x4, matrix products, chunk_stats(): lax.dot_general(normed, piece, (((1,), (1,)), ((), ())), preferred_elemen...  11 us
    unnamed x20, local copies, waits for them, and re-layouts  5.12 us
    reduce_sum x1, other arithmetic, chunk_stats(): jnp.sum(weights * shifted, axis=1)  3.9 us
  transfers between devices with their start and end apart: 8, of which 6 were waited for; matrix products, arithmetic and copies ran while one was open for 9% of the time, Pallas kernels for 0%

profile of v1, /device:TPU:1, one launch (start us, length us, event | category | flops | bytes accessed | tf_op | source)
XLA Modules:
  0.0 140.3 jit_solution(7402019807284296262)
XLA Ops:
  7.2 0.7 all-gather.2.cloned.1.call-update
  7.9 0.6 compare_reduce_fusion.1
  8.5 0.6 compare_reduce_fusion
  9.2 2.0 %broadcast_select_fusion = (bf16[128]{0:T(256)(128)(2,1)S(1)}, bf16[128,1]{0,1:T(2,128)(2,1)S(1)}) fusion(pred[]{:T(512)} %compare_reduce_fusion, s32[128]{0:T(128)} %param.12, pred[]{:T(512)} %compare_reduce_fusion.1), kind=kLoop, calls=%fused_computation.146 | loop fusion | flops 2944 | bytes 1026 | tf_op jit(solution)/shard_map/slice | solution.py:65
  11.2 1.2 fusion.12
  12.4 2.1 %constant_dynamic-update-slice_fusion = (bf16[1024,1600]{0,1:T(8,128)(2,1)}, bf16[128,1600]{0,1:T(8,128)(2,1)S(1)}) fusion(f32[1600]{0:T(1024)} %param.10, f32[128]{0:T(128)S(1)} %add_rsqrt_fusion, bf16[128,1600]{0,1:T(8,128)(2,1)} %param.9), kind=kLoop, calls=%fused_computation.37 | loop fusion | flops 819199 | bytes 1235712
  14.6 4.0 %collective-permute-start.3 = (bf16[128,1616]{0,1:T(8,128)(2,1)S(1)}, bf16[128,1616]{0,1:T(8,128)(2,1)S(1)}, u32[]{:S(2)}, u32[]{:S(2)}) collective-permute-start(bf16[128,1616]{0,1:T(8,128)(2,1)S(1)} %pad_maximum_fusion), channel_id=1, source_target_pairs={{0,1},{1,2},{2,3},{3,4},{4,5},{5,6},{6,7},{7,0},{8,9},{9,10},{10,1... | collective-permute-start | bytes 1241096 | tf_op jit(solution)/shard_map/ppermute | solution.py:22
  18.6 3.8 %collective-permute-start = (bf16[128,1616]{0,1:T(8,128)(2,1)S(1)}, bf16[128,1616]{0,1:T(8,128)(2,1)S(1)}, u32[]{:S(2)}, u32[]{:S(2)}) collective-permute-start(bf16[128,1616]{0,1:T(8,128)(2,1)S(1)} %pad_maximum_fusion), channel_id=1, source_target_pairs={{0,7},{1,0},{2,1},{3,2},{4,3},{5,4},{6,5},{7,6},{8,15},{9,8},{10,9... | collective-permute-start | bytes 1241096 | tf_op jit(solution)/shard_map/ppermute | solution.py:22
  22.5 3.4 %collective-permute-done.3 = bf16[128,1616]{0,1:T(8,128)(2,1)S(1)} collective-permute-done((bf16[128,1616]{0,1:T(8,128)(2,1)S(1)}, bf16[128,1616]{0,1:T(8,128)(2,1)S(1)}, u32[]{:S(2)}, u32[]{:S(2)}) %collective-permute-start.3) | collective-permute-done | bytes 413728 | tf_op jit(solution)/shard_map/ppermute | solution.py:22
  25.9 4.1 %collective-permute-start.4 = (bf16[128,1616]{0,1:T(8,128)(2,1)S(1)}, bf16[128,1616]{0,1:T(8,128)(2,1)S(1)}, u32[]{:S(2)}, u32[]{:S(2)}) collective-permute-start(bf16[128,1616]{0,1:T(8,128)(2,1)S(1)} %collective-permute-done.3), channel_id=1, source_target_pairs={{0,1},{1,2},{2,3},{3,4},{4,5},{5,6},{6,7},{7,0},{8,9},{9,10},{10,1... | collective-permute-start | bytes 1241096 | tf_op jit(solution)/shard_map/ppermute | solution.py:22
  30.0 4.7 %collective-permute-start.1 = (bf16[128,1616]{0,1:T(8,128)(2,1)S(1)}, bf16[128,1616]{0,1:T(8,128)(2,1)S(1)}, u32[]{:S(2)}, u32[]{:S(2)}) collective-permute-start(bf16[128,1616]{0,1:T(8,128)(2,1)S(1)} %collective-permute-done), channel_id=1, source_target_pairs={{0,7},{1,0},{2,1},{3,2},{4,3},{5,4},{6,5},{7,6},{8,15},{9,8},{10,9... | collective-permute-start | bytes 1241096 | tf_op jit(solution)/shard_map/ppermute | solution.py:22
  34.8 0.8 slice_dynamic-update-slice_fusion.6
  35.6 2.9 %collective-permute-done.4 = bf16[128,1616]{0,1:T(8,128)(2,1)S(1)} collective-permute-done((bf16[128,1616]{0,1:T(8,128)(2,1)S(1)}, bf16[128,1616]{0,1:T(8,128)(2,1)S(1)}, u32[]{:S(2)}, u32[]{:S(2)}) %collective-permute-start.4) | collective-permute-done | bytes 413728 | tf_op jit(solution)/shard_map/ppermute | solution.py:22
  38.5 2.9 %collective-permute-start.5 = (bf16[128,1616]{0,1:T(8,128)(2,1)S(1)}, bf16[128,1616]{0,1:T(8,128)(2,1)S(1)}, u32[]{:S(2)}, u32[]{:S(2)}) collective-permute-start(bf16[128,1616]{0,1:T(8,128)(2,1)S(1)} %collective-permute-done.4), channel_id=1, source_target_pairs={{0,1},{1,2},{2,3},{3,4},{4,5},{5,6},{6,7},{7,0},{8,9},{9,10},{10,1... | collective-permute-start | bytes 1241096 | tf_op jit(solution)/shard_map/ppermute | solution.py:22
  41.4 4.7 %collective-permute-start.2 = (bf16[128,1616]{0,1:T(8,128)(2,1)S(1)}, bf16[128,1616]{0,1:T(8,128)(2,1)S(1)}, u32[]{:S(2)}, u32[]{:S(2)}) collective-permute-start(bf16[128,1616]{0,1:T(8,128)(2,1)S(1)} %collective-permute-done.1), channel_id=1, source_target_pairs={{0,7},{1,0},{2,1},{3,2},{4,3},{5,4},{6,5},{7,6},{8,15},{9,8},{10,9... | collective-permute-start | bytes 1241096 | tf_op jit(solution)/shard_map/ppermute | solution.py:22
  46.1 0.9 slice_dynamic-update-slice_fusion.5
  47.0 2.9 %collective-permute-done.5 = bf16[128,1616]{0,1:T(8,128)(2,1)S(1)} collective-permute-done((bf16[128,1616]{0,1:T(8,128)(2,1)S(1)}, bf16[128,1616]{0,1:T(8,128)(2,1)S(1)}, u32[]{:S(2)}, u32[]{:S(2)}) %collective-permute-start.5) | collective-permute-done | bytes 413728 | tf_op jit(solution)/shard_map/ppermute | solution.py:22
  50.0 2.1 %collective-permute-start.6 = (bf16[128,1616]{0,1:T(8,128)(2,1)S(1)}, bf16[128,1616]{0,1:T(8,128)(2,1)S(1)}, u32[]{:S(2)}, u32[]{:S(2)}) collective-permute-start(bf16[128,1616]{0,1:T(8,128)(2,1)S(1)} %collective-permute-done.5), channel_id=1, source_target_pairs={{0,1},{1,2},{2,3},{3,4},{4,5},{5,6},{6,7},{7,0},{8,9},{9,10},{10,1... | collective-permute-start | bytes 1241096 | tf_op jit(solution)/shard_map/ppermute | solution.py:22
  52.1 2.0 %collective-permute-done.2 = bf16[128,1616]{0,1:T(8,128)(2,1)S(1)} collective-permute-done((bf16[128,1616]{0,1:T(8,128)(2,1)S(1)}, bf16[128,1616]{0,1:T(8,128)(2,1)S(1)}, u32[]{:S(2)}, u32[]{:S(2)}) %collective-permute-start.2) | collective-permute-done | bytes 413728 | tf_op jit(solution)/shard_map/ppermute | solution.py:22
  54.1 0.8 slice_dynamic-update-slice_fusion.4
  54.9 5.5 %collective-permute-done.6 = bf16[128,1616]{0,1:T(8,128)(2,1)S(1)} collective-permute-done((bf16[128,1616]{0,1:T(8,128)(2,1)S(1)}, bf16[128,1616]{0,1:T(8,128)(2,1)S(1)}, u32[]{:S(2)}, u32[]{:S(2)}) %collective-permute-start.6) | collective-permute-done | bytes 413728 | tf_op jit(solution)/shard_map/ppermute | solution.py:22
  60.5 0.8 slice_dynamic-update-slice_fusion.3
  61.4 0.9 slice_dynamic-update-slice_fusion.2
  62.2 0.8 slice_dynamic-update-slice_fusion.1
  63.1 0.9 slice_dynamic-update-slice_fusion
  63.9 40.9 %all-gather.2.cloned.1.call-done = bf16[2048,1600]{1,0:T(8,128)(2,1)} async-done(((bf16[32,1600]{1,0:T(8,128)(2,1)}), bf16[2048,1600]{1,0:T(8,128)(2,1)}) %all-gather.2.cloned.1.call-update) | async-done | bytes 6553616 | tf_op jit(solution)/shard_map/all_gather | solution.py:68
  104.8 4.7 %fusion.83 = (f32[1024]{0:T(1024)S(1)}, f32[1024,512]{0,1:T(8,128)S(1)}) fusion(bf16[1024,1600]{0,1:T(8,128)(2,1)} %slice_dynamic-update-slice_fusion, bf16[2048,1600]{1,0:T(8,128)(2,1)} %all-gather.2.cloned.1.call-done), kind=kOutput, calls=%fused_computation.195 | convolution fusion | flops 1678244864 | bytes 7081984 | tf_op jit(solution)/shard_map/dot_general | solution.py:26
  109.5 2.1 %fusion.84 = (f32[1024]{0:T(1024)S(1)}, f32[1024,512]{0,1:T(8,128)S(1)}) fusion(bf16[1024,1600]{0,1:T(8,128)(2,1)S(1)} %copy-done, bf16[2048,1600]{1,0:T(8,128)(2,1)S(1)} %copy-done.2), kind=kOutput, calls=%fused_computation.196 | convolution fusion | flops 1678244864 | bytes 7081984 | tf_op jit(solution)/shard_map/dot_general | solution.py:26
  111.7 2.1 %fusion.85 = (f32[1024]{0:T(1024)S(1)}, f32[1024,512]{0,1:T(8,128)S(1)}) fusion(bf16[1024,1600]{0,1:T(8,128)(2,1)S(1)} %copy-done, bf16[2048,1600]{1,0:T(8,128)(2,1)S(1)} %copy-done.2), kind=kOutput, calls=%fused_computation.197 | convolution fusion | flops 1678244864 | bytes 7081984 | tf_op jit(solution)/shard_map/dot_general | solution.py:26
  113.8 2.1 %fusion.86 = (f32[1024]{0:T(1024)S(1)}, f32[1024,512]{0,1:T(8,128)S(1)}) fusion(bf16[1024,1600]{0,1:T(8,128)(2,1)S(1)} %copy-done, bf16[2048,1600]{1,0:T(8,128)(2,1)S(1)} %copy-done.2), kind=kOutput, calls=%fused_computation.198 | convolution fusion | flops 1678244864 | bytes 7081984 | tf_op jit(solution)/shard_map/dot_general | solution.py:26
  115.9 3.9 %fusion = (f32[1024]{0:T(1024)S(1)}, f32[1024]{0:T(1024)S(1)}, f32[1024]{0:T(1024)S(1)}, f32[1024]{0:T(1024)S(1)}, f32[1024]{0:T(1024)S(1)}, /*index=5*/f32[1024...) fusion(f32[1024,512]{0,1:T(8,128)S(1)} %get-tuple-element.67, ...), kind=kLoop, calls=%fused_computation.8 | loop fusion | flops 14667776 | bytes 8466432 | tf_op jit(solution)/shard_map/reduce_sum | solution.py:33
  120.0 12.9 %all_to_all.5 = f32[8,4,128]{2,1,0:T(4,128)S(1)} all-to-all(f32[8,4,128]{2,1,0:T(4,128)S(1)} %constant_dynamic-update-slice_fusion.2), channel_id=1, replica_groups=mesh['z'=8,'x'=4,'c'=2,'y'=8] {'y'}, dimensions={0} | all-to-all | bytes 32768 | tf_op jit(solution)/shard_map/all_to_all | solution.py:81
  (40 shorter events, 1.0 us)
Async XLA Ops:
  7.2 97.7 %all-gather.2.cloned.1.call-start = ((), (), s32[]{:S(2)}) async-start(), calls=%async_computation.1 | async-start | bytes 6922240 | tf_op jit(solution)/shard_map/all_gather | solution.py:68
  14.6 11.3 %collective-permute-start.3 = (bf16[128,1616]{0,1:T(8,128)(2,1)S(1)}, bf16[128,1616]{0,1:T(8,128)(2,1)S(1)}, u32[]{:S(2)}, u32[]{:S(2)}) collective-permute-start(bf16[128,1616]{0,1:T(8,128)(2,1)S(1)} %pad_maximum_fusion), channel_id=1, source_target_pairs={{0,1},{1,2},{2,3},{3,4},{4,5},{5,6},{6,7},{7,0},{8,9},{9,10},{10,1... | collective-permute-start | bytes 1241096 | tf_op jit(solution)/shard_map/ppermute | solution.py:22
  18.6 11.4 %collective-permute-start = (bf16[128,1616]{0,1:T(8,128)(2,1)S(1)}, bf16[128,1616]{0,1:T(8,128)(2,1)S(1)}, u32[]{:S(2)}, u32[]{:S(2)}) collective-permute-start(bf16[128,1616]{0,1:T(8,128)(2,1)S(1)} %pad_maximum_fusion), channel_id=1, source_target_pairs={{0,7},{1,0},{2,1},{3,2},{4,3},{5,4},{6,5},{7,6},{8,15},{9,8},{10,9... | collective-permute-start | bytes 1241096 | tf_op jit(solution)/shard_map/ppermute | solution.py:22
  25.9 12.6 %collective-permute-start.4 = (bf16[128,1616]{0,1:T(8,128)(2,1)S(1)}, bf16[128,1616]{0,1:T(8,128)(2,1)S(1)}, u32[]{:S(2)}, u32[]{:S(2)}) collective-permute-start(bf16[128,1616]{0,1:T(8,128)(2,1)S(1)} %collective-permute-done.3), channel_id=1, source_target_pairs={{0,1},{1,2},{2,3},{3,4},{4,5},{5,6},{6,7},{7,0},{8,9},{9,10},{10,1... | collective-permute-start | bytes 1241096 | tf_op jit(solution)/shard_map/ppermute | solution.py:22
  30.0 11.4 %collective-permute-start.1 = (bf16[128,1616]{0,1:T(8,128)(2,1)S(1)}, bf16[128,1616]{0,1:T(8,128)(2,1)S(1)}, u32[]{:S(2)}, u32[]{:S(2)}) collective-permute-start(bf16[128,1616]{0,1:T(8,128)(2,1)S(1)} %collective-permute-done), channel_id=1, source_target_pairs={{0,7},{1,0},{2,1},{3,2},{4,3},{5,4},{6,5},{7,6},{8,15},{9,8},{10,9... | collective-permute-start | bytes 1241096 | tf_op jit(solution)/shard_map/ppermute | solution.py:22
  38.5 11.5 %collective-permute-start.5 = (bf16[128,1616]{0,1:T(8,128)(2,1)S(1)}, bf16[128,1616]{0,1:T(8,128)(2,1)S(1)}, u32[]{:S(2)}, u32[]{:S(2)}) collective-permute-start(bf16[128,1616]{0,1:T(8,128)(2,1)S(1)} %collective-permute-done.4), channel_id=1, source_target_pairs={{0,1},{1,2},{2,3},{3,4},{4,5},{5,6},{6,7},{7,0},{8,9},{9,10},{10,1... | collective-permute-start | bytes 1241096 | tf_op jit(solution)/shard_map/ppermute | solution.py:22
  41.4 12.7 %collective-permute-start.2 = (bf16[128,1616]{0,1:T(8,128)(2,1)S(1)}, bf16[128,1616]{0,1:T(8,128)(2,1)S(1)}, u32[]{:S(2)}, u32[]{:S(2)}) collective-permute-start(bf16[128,1616]{0,1:T(8,128)(2,1)S(1)} %collective-permute-done.1), channel_id=1, source_target_pairs={{0,7},{1,0},{2,1},{3,2},{4,3},{5,4},{6,5},{7,6},{8,15},{9,8},{10,9... | collective-permute-start | bytes 1241096 | tf_op jit(solution)/shard_map/ppermute | solution.py:22
  50.0 10.5 %collective-permute-start.6 = (bf16[128,1616]{0,1:T(8,128)(2,1)S(1)}, bf16[128,1616]{0,1:T(8,128)(2,1)S(1)}, u32[]{:S(2)}, u32[]{:S(2)}) collective-permute-start(bf16[128,1616]{0,1:T(8,128)(2,1)S(1)} %collective-permute-done.5), channel_id=1, source_target_pairs={{0,1},{1,2},{2,3},{3,4},{4,5},{5,6},{6,7},{7,0},{8,9},{9,10},{10,1... | collective-permute-start | bytes 1241096 | tf_op jit(solution)/shard_map/ppermute | solution.py:22
  63.9 45.6 %copy-start = (bf16[1024,1600]{0,1:T(8,128)(2,1)S(1)}, bf16[1024,1600]{0,1:T(8,128)(2,1)}, u32[]{:S(2)}) copy-start(bf16[1024,1600]{0,1:T(8,128)(2,1)} %slice_dynamic-update-slice_fusion) | copy-start | bytes 9830404
  104.8 4.7 %copy-start.2 = (bf16[2048,1600]{1,0:T(8,128)(2,1)S(1)}, bf16[2048,1600]{1,0:T(8,128)(2,1)}, u32[]{:S(2)}) copy-start(bf16[2048,1600]{1,0:T(8,128)(2,1)} %all-gather.2.cloned.1.call-done) | copy-start | bytes 19660804
  115.9 17.1 %copy-start.1 = (s32[128]{0:T(128)S(1)}, s32[128]{0:T(128)}, u32[]{:S(2)}) copy-start(s32[128]{0:T(128)} %param.13) | copy-start | bytes 1540
Sparse Core Ops, SparseCore 0:
  11.3 93.4 all-gather.1
